TPU v7x, 32 devices: a whole 2x2x4 slice. The times are simulated.
32 devices in a mesh: dp: 2 (over y), pipe: 4 (over z), tensor: 4 (over x, core).
Axes of the slice: x: 2, y: 2, z: 4, core: 2. Of those that a mesh axis runs over, the one named last changes fastest.
Arguments:
- kept_qkv: bfloat16 [2, 4, 3, 192, 6144], P('dp', 'pipe', None, None, 'tensor'), may hold values from -20 to 20
- held_qkv: bfloat16 [2, 4, 3, 192, 6144], P('dp', 'pipe', None, None, 'tensor'), may hold values from -20 to 20
- sent_grad: bfloat16 [2, 4, 2, 64, 6144], P('dp', 'pipe', None, 'tensor'), may hold values from -60 to 60
- order: int32 [2, 4], P('dp', 'pipe'), may hold values from 0 to 1
- offsets: int32 [2, 4, 2], P('dp'), may hold values from 0 to 128, as said below
Outputs:
- query_grad: bfloat16 [2, 4, 2, 64, 6144], P('dp', 'pipe', None, None, 'tensor')
- key_value_grad: bfloat16 [2, 4, 2, 2, 192, 6144], P('dp', 'pipe', None, None, None, 'tensor')
- bias_grad: float32 [4, 3, 6144], P('pipe', None, 'tensor')
Inputs may be any that keep to these rules, and one draw needn't show every extreme that they name: `offsets`: multiples of 64.
All inputs are finite; a program needn't handle non-finite values.
Results may differ from a plain program's by a relative error of at most 0.019.
Values may be sent and summed in bfloat16 or wider, within the bound.
No kernel may reach another device: no remote copies, remote signals or barrier semaphores. Data moves between devices by JAX's collectives and lax.ppermute only.
A program may use at most 64 MiB of HBM per device.

v0:
```python
import math
import jax
import jax.numpy as jnp
from jax import lax
from jax.sharding import PartitionSpec as P

HD = 128
MASK_FILL = -1e30


def from_behind(value, axis, steps):
    count = lax.axis_size(axis)
    pairs = [(source, (source + steps) % count) for source in range(count)]
    return lax.ppermute(value, axis, pairs)


def slice_backward(stash, grad_out, offset):
    key_count = stash.shape[1]
    row_count = grad_out.shape[0]
    feature_count = stash.shape[2]
    head_count = feature_count // HD
    score_scale = 1.0 / math.sqrt(HD)
    queries = lax.dynamic_slice_in_dim(stash[0], offset, row_count, 0).reshape(
        row_count, head_count, HD
    )
    key_rows = stash[1].reshape(key_count, head_count, HD)
    value_rows = stash[2].reshape(key_count, head_count, HD)
    out_grad = grad_out.reshape(row_count, head_count, HD)
    positions = offset + jnp.arange(row_count, dtype=jnp.int32)
    columns = jnp.arange(key_count, dtype=jnp.int32)
    visible = columns[None, :] <= positions[:, None]
    scores = (
        jnp.einsum("qhd,khd->hqk", queries, key_rows, preferred_element_type=jnp.float32)
        * score_scale
    )
    scores = jnp.where(visible[None], scores, MASK_FILL)
    row_max = jnp.max(scores, axis=-1, keepdims=True)
    expos = jnp.exp(scores - row_max)
    attention = expos / jnp.sum(expos, axis=-1, keepdims=True)
    attention_low = attention.astype(jnp.bfloat16)
    context = jnp.einsum(
        "hqk,khd->qhd", attention_low, value_rows, preferred_element_type=jnp.float32
    ).astype(jnp.bfloat16)
    delta = jnp.sum(out_grad.astype(jnp.float32) * context.astype(jnp.float32), axis=-1).T
    value_grad = jnp.einsum(
        "hqk,qhd->khd", attention_low, out_grad, preferred_element_type=jnp.float32
    ).astype(jnp.bfloat16)
    prob_grad = jnp.einsum("qhd,khd->hqk", out_grad, value_rows, preferred_element_type=jnp.float32)
    score_grad = (attention * (prob_grad - delta[:, :, None]) * score_scale).astype(jnp.bfloat16)
    query_grad = jnp.einsum(
        "hqk,khd->qhd", score_grad, key_rows, preferred_element_type=jnp.float32
    ).astype(jnp.bfloat16)
    key_grad = jnp.einsum(
        "hqk,qhd->khd", score_grad, queries, preferred_element_type=jnp.float32
    ).astype(jnp.bfloat16)
    both_grads = jnp.stack(
        [key_grad.reshape(key_count, feature_count), value_grad.reshape(key_count, feature_count)]
    )
    return (query_grad.reshape(row_count, feature_count), both_grads)


def body(kept_qkv, held_qkv, sent_grad, order, offsets):
    arrived = from_behind(sent_grad, "pipe", -1)
    regrouped = lax.all_to_all(arrived, "tensor", split_axis=4, concat_axis=3, tiled=True)
    kept_first = order[0, 0] == 0
    grad_kept = jnp.where(kept_first, regrouped[0, 0, 0], regrouped[0, 0, 1])
    grad_held = jnp.where(kept_first, regrouped[0, 0, 1], regrouped[0, 0, 0])
    section_index = lax.axis_index("pipe")
    section_count = lax.axis_size("pipe")
    half_way = section_count // 2
    section_offsets = lax.dynamic_index_in_dim(offsets[0], section_index, 0, keepdims=False)
    kept_q, kept_kv = slice_backward(kept_qkv[0, 0], grad_kept, section_offsets[0])
    fetched = from_behind(held_qkv[0, 0], "pipe", half_way)
    held_q, held_kv = slice_backward(fetched, grad_held, section_offsets[1])
    query_grad = jnp.stack([kept_q, held_q])
    key_value_grad = jnp.stack([kept_kv, held_kv])
    query_sums = jnp.sum(query_grad.astype(jnp.float32), axis=(0, 1))
    key_sums = jnp.sum(key_value_grad[:, 0].astype(jnp.float32), axis=(0, 1))
    value_sums = jnp.sum(key_value_grad[:, 1].astype(jnp.float32), axis=(0, 1))
    column_sums = jnp.stack([query_sums, key_sums, value_sums])
    bias_grad = lax.psum(column_sums, "dp")
    return (query_grad[None, None], key_value_grad[None, None], bias_grad[None])


def solution(mesh):
    return jax.shard_map(
        body,
        mesh=mesh,
        in_specs=(
            P("dp", "pipe", None, None, "tensor"),
            P("dp", "pipe", None, None, "tensor"),
            P("dp", "pipe", None, "tensor", None),
            P("dp", "pipe"),
            P("dp", None, None),
        ),
        out_specs=(
            P("dp", "pipe", None, None, "tensor"),
            P("dp", "pipe", None, None, None, "tensor"),
            P("pipe", None, "tensor"),
        ),
        check_vma=False,
    )
```

profile of v0, /device:TPU:8, one launch (start us, length us, event | category | flops | bytes accessed | tf_op | source)
XLA Modules:
  0.0 121.3 jit_solution(14244090203486681753)
XLA Ops:
  0.7 3.0 %collective-permute-start.1 = (bf16[3,192,1536]{2,1,0:T(8,128)(2,1)}, bf16[3,192,1536]{2,1,0:T(8,128)(2,1)}, u32[]{:S(2)}, u32[]{:S(2)}) collective-permute-start(bf16[3,192,1536]{2,1,0:T(8,128)(2,1)} %bitcast.67), channel_id=1, source_target_pairs={{0,8},{4,12},{8,0},{12,4},{1,9},{5,13},{9,1},{13,5},{2,10},{6,14},... | collective-permute-start | bytes 5308424 | tf_op jit(solution)/shard_map/ppermute | solution.py:14
  3.8 0.5 fusion.55
  4.4 0.6 iota_add_fusion.1
  5.7 2.4 %fusion.54 = (bf16[1,1,1,192,1536]{4,3,2,1,0:T(8,128)(2,1)S(1)}, bf16[1,1,1,192,1536]{4,3,2,1,0:T(8,128)(2,1)}, bf16[1,1,1,192,1536]{4,3,2,1,0:T(8,128)(2,1)S(1)}) fusion(bf16[1,1,3,192,1536]{4,3,2,1,0:T(8,128)(2,1)} %param.5), kind=kLoop, calls=%fused_computation.86 | loop fusion | bytes 3538944 | tf_op jit(solution)/shard_map/slice | solution.py:23
  10.1 0.6 iota_add_fusion
  10.7 1.4 %fusion.7 = f32[12,64,192]{2,1,0:T(8,128)} fusion(bf16[192,12,128]{2,1,0:T(8,128)(2,1)S(1)} %reshape_squeeze.12, pred[64,192]{1,0:T(8,128)(4,1)S(1)} %iota_compare_fusion.1, bf16[64,12,128]{2,1,0:T(8,128)(2,1)S(1)} %reshape.94), kind=kOutput, calls=%fused_computation.22 | convolution fusion | flops 38043648 | bytes 1388544 | tf_op jit(solution)/shard_map/qhd,khd->hqk/dot_general | solution.py:33
  12.1 38.8 %collective-permute-done = bf16[1,1,2,16,6144]{4,3,2,1,0:T(8,128)(2,1)} collective-permute-done((bf16[1,1,2,16,6144]{4,3,2,1,0:T(8,128)(2,1)}, bf16[1,1,2,16,6144]{4,3,2,1,0:T(8,128)(2,1)}, u32[]{:S(2)}, u32[]{:S(2)}) %collective-permute-start) | collective-permute-done | bytes 393248 | tf_op jit(solution)/shard_map/ppermute | solution.py:14
  50.9 6.1 %copy.86 = bf16[1,1,2,16,6144]{3,2,1,0,4:T(2,128)(2,1)S(1)} copy(bf16[1,1,2,16,6144]{4,3,2,1,0:T(8,128)(2,1)} %collective-permute-done) | data formatting | bytes 786432 | tf_op jit(solution)/shard_map/ppermute | solution.py:14
  57.0 4.0 %reshape.96 = bf16[4,2,24576]{2,1,0:T(2,128)(2,1)} reshape(bf16[6144,1,1,2,16]{4,3,2,1,0:T(2,128)(2,1)S(1)} %bitcast.62) | data formatting | bytes 786432
  61.0 4.2 %all-to-all-start = ((bf16[4,2,24576]{2,1,0:T(2,128)(2,1)}), bf16[4,2,24576]{2,1,0:T(2,128)(2,1)}, u32[]{:S(2)}, u32[]{:S(2)}) async-start(bf16[4,2,24576]{2,1,0:T(2,128)(2,1)} %reshape.96), calls=%async_computation | async-start | bytes 786432 | tf_op jit(solution)/shard_map/all_to_all | solution.py:64
  66.6 2.2 %reshape_squeeze.13 = bf16[192,12,128]{2,1,0:T(8,128)(2,1)} reshape(bf16[1,1,1,192,1536]{4,3,2,1,0:T(8,128)(2,1)} %get-tuple-element.9) | data formatting | bytes 1179648 | tf_op jit(solution)/shard_map/reshape;squeeze | solution.py:27
  70.1 1.1 fusion.56
  71.2 1.5 %all-to-all-done = bf16[4,2,24576]{2,1,0:T(2,128)(2,1)} async-done(((bf16[4,2,24576]{2,1,0:T(2,128)(2,1)}), bf16[4,2,24576]{2,1,0:T(2,128)(2,1)}, u32[]{:S(2)}, u32[]{:S(2)}) %all-to-all-start) | async-done | bytes 393248 | tf_op jit(solution)/shard_map/all_to_all | solution.py:64
  72.7 3.5 %reshape.97 = bf16[6144,1,1,2,16]{4,3,2,1,0:T(2,128)(2,1)S(1)} reshape(bf16[4,2,24576]{2,1,0:T(2,128)(2,1)} %all-to-all-done) | data formatting | bytes 786432
  76.2 4.8 %copy.111 = bf16[1,1,2,16,4,1536]{5,4,3,2,1,0:T(4,128)(2,1)} copy(bf16[1,1,2,16,4,1536]{3,2,5,4,1,0:T(2,128)(2,1)S(1)} %bitcast.63) | data formatting | bytes 786432 | tf_op jit(solution)/shard_map/all_to_all | solution.py:64
  81.1 1.1 copy.88
  82.4 3.0 %fusion.27 = f32[64,12]{0,1:T(8,128)S(1)} fusion(bf16[192,12,128]{2,1,0:T(8,128)(2,1)S(1)} %copy-done.8, bf16[64,12,128]{2,1,0:T(8,128)(2,1)S(1)} %select_n.42, f32[12,64]{1,0:T(8,128)S(1)} %get-tuple-element.15, f32[12,64,192]{2,1,0:T(8,128)} %fusion.7), kind=kOutput, calls=%fused_computation.48 | convolution fusion | flops 38682816 | bytes 1382400 | tf_op jit(solution)/shard_map/hqk,khd->qhd/dot_general | solution.py:41
  85.4 0.5 fusion.14
  85.9 0.6 copy-done.2
  87.2 0.8 select_n.46
  88.0 3.1 %fusion.16 = bf16[192,12,128]{2,0,1:T(8,128)(2,1)S(1)} fusion(bf16[64,12,128]{2,1,0:T(8,128)(2,1)S(1)} %select_n.42, f32[12,64]{1,0:T(8,128)S(1)} %get-tuple-element.15, f32[12,64,192]{2,1,0:T(8,128)} %fusion.7), kind=kOutput, calls=%fused_computation.31 | convolution fusion | flops 38486976 | bytes 1379328 | tf_op jit(solution)/shard_map/hqk,qhd->khd/dot_general | solution.py:45
  93.1 0.7 constant_dynamic-update-slice_fusion.1
  93.8 1.5 %fusion.53 = (bf16[1,192,1536]{2,1,0:T(8,128)(2,1)S(1)}, bf16[1,192,1536]{2,1,0:T(8,128)(2,1)S(1)}, bf16[1,192,1536]{2,1,0:T(8,128)(2,1)S(1)}) fusion(bf16[3,192,1536]{2,1,0:T(8,128)(2,1)} %collective-permute-done.1), kind=kLoop, calls=%fused_computation.85 | loop fusion | bytes 3538944 | tf_op jit(solution)/shard_map/slice | solution.py:23
  95.4 1.3 %reshape_squeeze.15 = bf16[192,12,128]{2,1,0:T(8,128)(2,1)} reshape(bf16[1,192,1536]{2,1,0:T(8,128)(2,1)S(1)} %get-tuple-element.6) | data formatting | bytes 1179648 | tf_op jit(solution)/shard_map/reshape;squeeze | solution.py:27
  97.8 1.1 fusion.57
  98.9 2.5 %fusion.18 = bf16[192,12,128]{2,0,1:T(8,128)(2,1)} fusion(bf16[64,12,128]{2,1,0:T(8,128)(2,1)S(1)} %copy-done.10, f32[12,64]{1,0:T(8,128)S(1)} %get-tuple-element.17, f32[12,64,192]{2,1,0:T(8,128)S(1)} %fusion.10), kind=kOutput, calls=%fused_computation.33 | convolution fusion | flops 38486976 | bytes 1379328 | tf_op jit(solution)/shard_map/hqk,qhd->khd/dot_general | solution.py:45
  101.4 2.7 %fusion.28 = f32[64,12]{0,1:T(8,128)S(1)} fusion(bf16[192,12,128]{2,1,0:T(8,128)(2,1)} %reshape_squeeze.15, bf16[64,12,128]{2,1,0:T(8,128)(2,1)S(1)} %copy-done.10, f32[12,64]{1,0:T(8,128)S(1)} %get-tuple-element.17, f32[12,64,192]{2,1,0:T(8,128)S(1)} %fusion.10), kind=kOutput, calls=%fused_computation.49 | convolution fusion | flops 38682816 | bytes 1382400 | tf_op jit(solution)/shard_map/hqk,khd->qhd/dot_general | solution.py:41
  104.1 1.9 %fusion.13 = bf16[12,64,192]{2,1,0:T(8,128)(2,1)S(1)} fusion(bf16[192,12,128]{2,1,0:T(8,128)(2,1)} %reshape_squeeze.15, f32[12,64]{1,0:T(8,128)S(1)} %bitcast.68, f32[12,64,192]{2,1,0:T(8,128)} %get-tuple-element.18, f32[12,64]{1,0:T(8,128)S(1)} %get-tuple-element.17, bf16[64,12,128]{2,1,0:T(8,128)(2,1)S(1)} %copy-done.10), kind=kOutput, calls=%fused_computation.28 | convolution fusion | flops 38486016 | bytes 1677312 | tf_op jit(solution)/shard_map/qhd,khd->hqk/dot_general | solution.py:48
  106.0 1.0 fusion.30
  109.2 1.6 %fusion.2 = bf16[1,1,2,2,192,1536]{5,4,3,2,1,0:T(8,128)(2,1)} fusion(bf16[1,2,192,1536]{3,2,1,0:T(8,128)(2,1)S(1)} %get-tuple-element.20, bf16[1,2,192,1536]{3,2,1,0:T(8,128)(2,1)S(1)} %get-tuple-element.19), kind=kLoop, calls=%fused_computation.7 | loop fusion | flops 1179648 | bytes 4718592 | tf_op jit(solution)/shard_map/broadcast_in_dim | solution.py:82
  111.2 0.5 copy-done.6
  112.3 9.0 %psum.7 = f32[1,3,1536]{2,0,1:T(1,128)} all-reduce(f32[1,3,1536]{2,0,1:T(1,128)S(1)} %broadcast_in_dim.44), channel_id=1, replica_groups=mesh['dp'=2,'pipe'=4,'tensor'=4] {'dp'}, use_global_device_ids=true, to_apply=%region_9.10 | all-reduce | flops 4608 | bytes 36864 | tf_op jit(solution)/shard_map/psum | solution.py:81
  (58 shorter events, 7.9 us)
Async XLA Ops:
  0.6 3.1 %copy-start = (s32[1,4,2]{1,2,0:T(2,128)S(1)}, s32[1,4,2]{1,2,0:T(2,128)}, u32[]{:S(2)}) copy-start(s32[1,4,2]{1,2,0:T(2,128)} %param.9) | copy-start | bytes 100
  0.6 50.3 %collective-permute-start = (bf16[1,1,2,16,6144]{4,3,2,1,0:T(8,128)(2,1)}, bf16[1,1,2,16,6144]{4,3,2,1,0:T(8,128)(2,1)}, u32[]{:S(2)}, u32[]{:S(2)}) collective-permute-start(bf16[1,1,2,16,6144]{4,3,2,1,0:T(8,128)(2,1)} %param.7), channel_id=1, source_target_pairs={{0,12},{4,0},{8,4},{12,8},{1,13},{5,1},{9,5},{13,9},{2,14},{6,2},{... | collective-permute-start | bytes 1179656 | tf_op jit(solution)/shard_map/ppermute | solution.py:14
  0.7 93.1 %collective-permute-start.1 = (bf16[3,192,1536]{2,1,0:T(8,128)(2,1)}, bf16[3,192,1536]{2,1,0:T(8,128)(2,1)}, u32[]{:S(2)}, u32[]{:S(2)}) collective-permute-start(bf16[3,192,1536]{2,1,0:T(8,128)(2,1)} %bitcast.67), channel_id=1, source_target_pairs={{0,8},{4,12},{8,0},{12,4},{1,9},{5,13},{9,1},{13,5},{2,10},{6,14},... | collective-permute-start | bytes 5308424 | tf_op jit(solution)/shard_map/ppermute | solution.py:14
  9.9 2.2 %copy-start.1 = (bf16[192,12,128]{2,1,0:T(8,128)(2,1)}, bf16[192,12,128]{2,1,0:T(8,128)(2,1)S(1)}, u32[]{:S(2)}) copy-start(bf16[192,12,128]{2,1,0:T(8,128)(2,1)S(1)} %reshape_squeeze.12) | copy-start | bytes 1769476
  61.0 9.1 %copy-start.3 = (f32[12,64,192]{2,1,0:T(8,128)S(1)}, f32[12,64,192]{2,1,0:T(8,128)}, u32[]{:S(2)}) copy-start(f32[12,64,192]{2,1,0:T(8,128)} %fusion.7) | copy-start | bytes 1769476
  61.0 11.7 %all-to-all-start = ((bf16[4,2,24576]{2,1,0:T(2,128)(2,1)}), bf16[4,2,24576]{2,1,0:T(2,128)(2,1)}, u32[]{:S(2)}, u32[]{:S(2)}) async-start(bf16[4,2,24576]{2,1,0:T(2,128)(2,1)} %reshape.96), calls=%async_computation | async-start | bytes 786432 | tf_op jit(solution)/shard_map/all_to_all | solution.py:64
  81.1 1.3 %copy-start.8 = (bf16[192,12,128]{2,1,0:T(8,128)(2,1)S(1)}, bf16[192,12,128]{2,1,0:T(8,128)(2,1)}, u32[]{:S(2)}) copy-start(bf16[192,12,128]{2,1,0:T(8,128)(2,1)} %reshape_squeeze.13) | copy-start | bytes 1769476
  82.4 3.0 %copy-start.7 = (f32[12,64,192]{2,1,0:T(8,128)S(1)}, f32[12,64,192]{2,1,0:T(8,128)}, u32[]{:S(2)}) copy-start(f32[12,64,192]{2,1,0:T(8,128)} %get-tuple-element.16) | copy-start | bytes 1769476
  85.4 1.1 copy-start.2
  97.8 1.1 copy-start.10
  106.0 1.4 %copy-start.9 = (bf16[192,12,128]{2,0,1:T(8,128)(2,1)S(1)}, bf16[192,12,128]{2,0,1:T(8,128)(2,1)}, u32[]{:S(2)}) copy-start(bf16[192,12,128]{2,0,1:T(8,128)(2,1)} %fusion.18) | copy-start | bytes 1769476
  110.8 0.9 copy-start.6
  110.9 1.2 %copy-start.4 = (bf16[2,64,1536]{2,1,0:T(8,128)(2,1)S(1)}, bf16[2,64,1536]{2,1,0:T(8,128)(2,1)}, u32[]{:S(2)}) copy-start(bf16[2,64,1536]{2,1,0:T(8,128)(2,1)} %constant_dynamic-update-slice_fusion.1) | copy-start | bytes 1179652
  112.1 9.2 %copy-start.5 = (bf16[2,64,1536]{2,1,0:T(8,128)(2,1)}, bf16[2,64,1536]{2,1,0:T(8,128)(2,1)S(1)}, u32[]{:S(2)}) copy-start(bf16[2,64,1536]{2,1,0:T(8,128)(2,1)S(1)} %constant_dynamic-update-slice_fusion) | copy-start | bytes 1179652
where the time goes:
time: 122 us; the launch traced here: 121 us
  waiting for transfers between devices  40.4 us (33%)
  local copies, waits for them, and re-layouts  35.5 us (29%)
  matrix products  17.6 us (14%)
  blocking collectives  9.02 us (7%)
  starting transfers between devices  7.32 us (6%)
  other arithmetic  5.92 us (5%)
  between operations  5.53 us (5%)
    ppermute x2, waiting for transfers between devices, from_behind(): return lax.ppermute(value, axis, pairs)  38.8 us
    unnamed x25, local copies, waits for them, and re-layouts  9.33 us
    psum x1, blocking collectives, body(): bias_grad = lax.psum(column_sums, 'dp')  9.02 us
    ppermute x1, local copies, waits for them, and re-layouts, from_behind(): return lax.ppermute(value, axis, pairs)  6.09 us
    all_to_all x2, local copies, waits for them, and re-layouts, body(): lax.all_to_all(arrived, 'tensor', split_axis=4, concat_axis=3, tiled=True)  5.98 us
    dot_general x2, matrix products, slice_backward(): jnp.einsum('hqk,khd->qhd', attention_low, value_rows, preferred_element_t...  5.64 us
    dot_general x2, matrix products, slice_backward(): jnp.einsum('hqk,qhd->khd', attention_low, out_grad, preferred_element_typ...  5.59 us
    all_to_all x1, starting transfers between devices, body(): lax.all_to_all(arrived, 'tensor', split_axis=4, concat_axis=3, tiled=True)  4.24 us
  transfers between devices with their start and end apart: 3, of which 2 were waited for; matrix products, arithmetic and copies ran while one was open for 33% of the time, Pallas kernels for 0%

commit v1 on v0

--- a/solution.py
+++ b/solution.py
@@ -61,7 +61,9 @@
 
 def body(kept_qkv, held_qkv, sent_grad, order, offsets):
     arrived = from_behind(sent_grad, "pipe", -1)
-    regrouped = lax.all_to_all(arrived, "tensor", split_axis=4, concat_axis=3, tiled=True)
+    parts = jnp.split(arrived, lax.axis_size("tensor"), axis=4)
+    received = lax.all_to_all(jnp.stack(parts), "tensor", 0, 0)
+    regrouped = jnp.concatenate(received, axis=3)
     kept_first = order[0, 0] == 0
     grad_kept = jnp.where(kept_first, regrouped[0, 0, 0], regrouped[0, 0, 1])
     grad_held = jnp.where(kept_first, regrouped[0, 0, 1], regrouped[0, 0, 0])

time: 122 us -> 117 us (0.959)
  the two profiles are of different devices: /device:TPU:8 before, /device:TPU:0 now
where the time goes in v1:
time: 117 us
  waiting for transfers between devices  58.3 us (50%)
  matrix products  15.8 us (14%)
  local copies, waits for them, and re-layouts  12.8 us (11%)
  blocking collectives  8.89 us (8%)
  starting transfers between devices  8.56 us (7%)
  other arithmetic  6.69 us (6%)
  between operations  5.51 us (5%)
    ppermute x2, waiting for transfers between devices, from_behind(): return lax.ppermute(value, axis, pairs)  55.9 us
    psum x1, blocking collectives, body(): bias_grad = lax.psum(column_sums, 'dp')  8.89 us
    dot_general x2, matrix products, slice_backward(): jnp.einsum('hqk,khd->qhd', attention_low, value_rows, preferred_element_t...  5.45 us
    ppermute x2, starting transfers between devices, from_behind(): return lax.ppermute(value, axis, pairs)  5.1 us
    dot_general x2, matrix products, slice_backward(): jnp.einsum('hqk,qhd->khd', attention_low, out_grad, preferred_element_typ...  4.22 us
    dot_general x2, matrix products, slice_backward(): jnp.einsum('qhd,khd->hqk', out_grad, value_rows, preferred_element_type=j...  3.62 us
    all_to_all x1, starting transfers between devices, body(): received = lax.all_to_all(jnp.stack(parts), 'tensor', 0, 0)  3.46 us
    slice x2, local copies, waits for them, and re-layouts, slice_backward(): stash[0]  3.07 us
  transfers between devices with their start and end apart: 3, of which 3 were waited for; matrix products, arithmetic and copies ran while one was open for 15% of the time, Pallas kernels for 0%

profile of v1, /device:TPU:0, one launch (start us, length us, event | category | flops | bytes accessed | tf_op | source)
XLA Modules:
  0.0 116.5 jit_solution(17221263920328095458)
XLA Ops:
  0.6 5.1 %collective-permute-start = (bf16[1,1,2,16,6144]{4,3,2,1,0:T(8,128)(2,1)}, bf16[1,1,2,16,6144]{4,3,2,1,0:T(8,128)(2,1)S(1)}, u32[]{:S(2)}, u32[]{:S(2)}) collective-permute-start(bf16[1,1,2,16,6144]{4,3,2,1,0:T(8,128)(2,1)} %param.7), channel_id=1, source_target_pairs={{0,12},{4,0},{8,4},{12,8},{1,13},{5,1},{9,5},{13,9},{2,14},{6,2},{... | collective-permute-start | bytes 1179656 | tf_op jit(solution)/shard_map/ppermute | solution.py:14
  5.8 0.5 fusion.55
  7.0 0.6 iota_add_fusion.1
  8.3 1.5 %fusion.54 = (bf16[1,1,1,192,1536]{4,3,2,1,0:T(8,128)(2,1)S(1)}, bf16[1,1,1,192,1536]{4,3,2,1,0:T(8,128)(2,1)S(1)}, bf16[1,1,1,192,1536]{4,3,2,1,0:T(8,128)(2,1)S(1)}) fusion(bf16[1,1,3,192,1536]{4,3,2,1,0:T(8,128)(2,1)} %param.5), kind=kLoop, calls=%fused_computation.91 | loop fusion | bytes 3538944 | tf_op jit(solution)/shard_map/slice | solution.py:23
  10.8 0.4 reshape_squeeze.12
  11.2 0.6 iota_add_fusion
  11.9 0.5 fusion.7
  12.4 3.2 %collective-permute-done = bf16[1,1,2,16,6144]{4,3,2,1,0:T(8,128)(2,1)S(1)} collective-permute-done((bf16[1,1,2,16,6144]{4,3,2,1,0:T(8,128)(2,1)}, bf16[1,1,2,16,6144]{4,3,2,1,0:T(8,128)(2,1)S(1)}, u32[]{:S(2)}, u32[]{:S(2)}) %collective-permute-start) | collective-permute-done | bytes 393248 | tf_op jit(solution)/shard_map/ppermute | solution.py:14
  15.6 0.8 pad_maximum_fusion.1
  16.4 3.5 %all-to-all-start = ((bf16[4,1,1,2,16,1536]{5,4,3,2,1,0:T(8,128)(2,1)}), bf16[4,1,1,2,16,1536]{5,4,3,2,1,0:T(8,128)(2,1)S(1)}, u32[]{:S(2)}, u32[]{:S(2)}) async-start(bf16[4,1,1,2,16,1536]{5,4,3,2,1,0:T(8,128)(2,1)} %pad_maximum_fusion.1), calls=%async_computation | async-start | bytes 786432 | tf_op jit(solution)/shard_map/all_to_all | solution.py:65
  21.9 1.3 %reshape_squeeze.13 = bf16[192,12,128]{2,1,0:T(8,128)(2,1)} reshape(bf16[1,1,1,192,1536]{4,3,2,1,0:T(8,128)(2,1)S(1)} %get-tuple-element.9) | data formatting | bytes 1179648 | tf_op jit(solution)/shard_map/reshape;squeeze | solution.py:27
  23.8 1.1 fusion.56
  24.9 2.4 %all-to-all-done = bf16[4,1,1,2,16,1536]{5,4,3,2,1,0:T(8,128)(2,1)S(1)} async-done(((bf16[4,1,1,2,16,1536]{5,4,3,2,1,0:T(8,128)(2,1)}), bf16[4,1,1,2,16,1536]{5,4,3,2,1,0:T(8,128)(2,1)S(1)}, u32[]{:S(2)}, u32[]{:S(2)}) %all-to-all-start) | async-done | bytes 393248 | tf_op jit(solution)/shard_map/all_to_all | solution.py:65
  27.7 2.8 %fusion.27 = f32[64,12]{0,1:T(8,128)S(1)} fusion(bf16[192,12,128]{2,1,0:T(8,128)(2,1)} %reshape_squeeze.13, bf16[64,12,128]{2,1,0:T(8,128)(2,1)S(1)} %select_n.42, f32[12,64]{1,0:T(8,128)S(1)} %get-tuple-element.19, f32[12,64,192]{2,1,0:T(8,128)S(1)} %fusion.7), kind=kOutput, calls=%fused_computation.48 | convolution fusion | flops 38682816 | bytes 1382400 | tf_op jit(solution)/shard_map/hqk,khd->qhd/dot_general | solution.py:41
  30.5 1.7 %fusion.14 = bf16[12,64,192]{2,1,0:T(8,128)(2,1)S(1)} fusion(bf16[192,12,128]{2,1,0:T(8,128)(2,1)} %reshape_squeeze.13, f32[12,64]{1,0:T(8,128)S(1)} %bitcast.72, f32[12,64,192]{2,1,0:T(8,128)S(1)} %copy-done.3, f32[12,64]{1,0:T(8,128)S(1)} %get-tuple-element.19, bf16[64,12,128]{2,1,0:T(8,128)(2,1)} %copy-done.5), kind=kOutput, calls=%fused_computation.29 | convolution fusion | flops 38486016 | bytes 1677312 | tf_op jit(solution)/shard_map/qhd,khd->hqk/dot_general | solution.py:48
  33.3 0.4 copy.53
  34.2 1.7 %fusion.16 = bf16[192,12,128]{2,0,1:T(8,128)(2,1)S(1)} fusion(bf16[64,12,128]{2,1,0:T(8,128)(2,1)S(1)} %copy-done.6, f32[12,64]{1,0:T(8,128)S(1)} %get-tuple-element.19, f32[12,64,192]{2,1,0:T(8,128)S(1)} %fusion.7), kind=kOutput, calls=%fused_computation.31 | convolution fusion | flops 38486976 | bytes 1379328 | tf_op jit(solution)/shard_map/hqk,qhd->khd/dot_general | solution.py:45
  35.9 0.4 copy.55
  36.8 0.7 constant_dynamic-update-slice_fusion.1
  37.4 52.7 %collective-permute-done.1 = bf16[3,192,1536]{2,1,0:T(8,128)(2,1)} collective-permute-done((bf16[3,192,1536]{2,1,0:T(8,128)(2,1)}, bf16[3,192,1536]{2,1,0:T(8,128)(2,1)}, u32[]{:S(2)}, u32[]{:S(2)}) %collective-permute-start.1) | collective-permute-done | bytes 1769504 | tf_op jit(solution)/shard_map/ppermute | solution.py:14
  90.2 1.5 %fusion.53 = (bf16[1,192,1536]{2,1,0:T(8,128)(2,1)S(1)}, bf16[1,192,1536]{2,1,0:T(8,128)(2,1)S(1)}, bf16[1,192,1536]{2,1,0:T(8,128)(2,1)S(1)}) fusion(bf16[3,192,1536]{2,1,0:T(8,128)(2,1)} %collective-permute-done.1), kind=kLoop, calls=%fused_computation.90 | loop fusion | bytes 3538944 | tf_op jit(solution)/shard_map/slice | solution.py:23
  91.9 1.3 %reshape_squeeze.15 = bf16[192,12,128]{2,1,0:T(8,128)(2,1)} reshape(bf16[1,192,1536]{2,1,0:T(8,128)(2,1)S(1)} %get-tuple-element.6) | data formatting | bytes 1179648 | tf_op jit(solution)/shard_map/reshape;squeeze | solution.py:27
  93.2 0.4 reshape_squeeze.14
  93.6 0.5 fusion.10
  94.1 1.1 fusion.57
  95.2 2.5 %fusion.18 = bf16[192,12,128]{2,0,1:T(8,128)(2,1)} fusion(bf16[64,12,128]{2,1,0:T(8,128)(2,1)S(1)} %select_n.46, f32[12,64]{1,0:T(8,128)S(1)} %get-tuple-element.21, f32[12,64,192]{2,1,0:T(8,128)S(1)} %fusion.10), kind=kOutput, calls=%fused_computation.33 | convolution fusion | flops 38486976 | bytes 1379328 | tf_op jit(solution)/shard_map/hqk,qhd->khd/dot_general | solution.py:45
  97.7 2.7 %fusion.28 = f32[64,12]{0,1:T(8,128)S(1)} fusion(bf16[192,12,128]{2,1,0:T(8,128)(2,1)} %reshape_squeeze.15, bf16[64,12,128]{2,1,0:T(8,128)(2,1)S(1)} %select_n.46, f32[12,64]{1,0:T(8,128)S(1)} %get-tuple-element.21, f32[12,64,192]{2,1,0:T(8,128)S(1)} %fusion.10), kind=kOutput, calls=%fused_computation.49 | convolution fusion | flops 38682816 | bytes 1382400 | tf_op jit(solution)/shard_map/hqk,khd->qhd/dot_general | solution.py:41
  100.4 1.9 %fusion.13 = bf16[12,64,192]{2,1,0:T(8,128)(2,1)S(1)} fusion(bf16[192,12,128]{2,1,0:T(8,128)(2,1)} %reshape_squeeze.15, f32[12,64]{1,0:T(8,128)S(1)} %bitcast.71, f32[12,64,192]{2,1,0:T(8,128)} %get-tuple-element.22, f32[12,64]{1,0:T(8,128)S(1)} %get-tuple-element.21, bf16[64,12,128]{2,1,0:T(8,128)(2,1)S(1)} %select_n.46), kind=kOutput, calls=%fused_computation.28 | convolution fusion | flops 38486016 | bytes 1677312 | tf_op jit(solution)/shard_map/qhd,khd->hqk/dot_general | solution.py:48
  103.0 0.4 copy.57
  104.1 0.4 copy.59
  105.5 1.6 %fusion.2 = bf16[1,1,2,2,192,1536]{5,4,3,2,1,0:T(8,128)(2,1)} fusion(bf16[1,2,192,1536]{3,2,1,0:T(8,128)(2,1)S(1)} %get-tuple-element.24, bf16[1,2,192,1536]{3,2,1,0:T(8,128)(2,1)S(1)} %get-tuple-element.23), kind=kLoop, calls=%fused_computation.7 | loop fusion | flops 1179648 | bytes 4718592 | tf_op jit(solution)/shard_map/broadcast_in_dim | solution.py:84
  107.6 8.9 %psum.7 = f32[1,3,1536]{2,0,1:T(1,128)} all-reduce(f32[1,3,1536]{2,0,1:T(1,128)S(1)} %broadcast_in_dim.44), channel_id=1, replica_groups=mesh['dp'=2,'pipe'=4,'tensor'=4] {'dp'}, use_global_device_ids=true, to_apply=%region_9.10 | all-reduce | flops 4608 | bytes 36864 | tf_op jit(solution)/shard_map/psum | solution.py:83
  (48 shorter events, 5.8 us)
Async XLA Ops:
  0.6 5.1 %copy-start = (s32[1,4,2]{1,2,0:T(2,128)S(1)}, s32[1,4,2]{1,2,0:T(2,128)}, u32[]{:S(2)}) copy-start(s32[1,4,2]{1,2,0:T(2,128)} %param.9) | copy-start | bytes 100
  0.6 14.9 %collective-permute-start = (bf16[1,1,2,16,6144]{4,3,2,1,0:T(8,128)(2,1)}, bf16[1,1,2,16,6144]{4,3,2,1,0:T(8,128)(2,1)S(1)}, u32[]{:S(2)}, u32[]{:S(2)}) collective-permute-start(bf16[1,1,2,16,6144]{4,3,2,1,0:T(8,128)(2,1)} %param.7), channel_id=1, source_target_pairs={{0,12},{4,0},{8,4},{12,8},{1,13},{5,1},{9,5},{13,9},{2,14},{6,2},{... | collective-permute-start | bytes 1179656 | tf_op jit(solution)/shard_map/ppermute | solution.py:14
  5.7 84.4 %collective-permute-start.1 = (bf16[3,192,1536]{2,1,0:T(8,128)(2,1)}, bf16[3,192,1536]{2,1,0:T(8,128)(2,1)}, u32[]{:S(2)}, u32[]{:S(2)}) collective-permute-start(bf16[3,192,1536]{2,1,0:T(8,128)(2,1)} %bitcast.70), channel_id=1, source_target_pairs={{0,8},{4,12},{8,0},{12,4},{1,9},{5,13},{9,1},{13,5},{2,10},{6,14},... | collective-permute-start | bytes 5308424 | tf_op jit(solution)/shard_map/ppermute | solution.py:14
  16.4 10.9 %all-to-all-start = ((bf16[4,1,1,2,16,1536]{5,4,3,2,1,0:T(8,128)(2,1)}), bf16[4,1,1,2,16,1536]{5,4,3,2,1,0:T(8,128)(2,1)S(1)}, u32[]{:S(2)}, u32[]{:S(2)}) async-start(bf16[4,1,1,2,16,1536]{5,4,3,2,1,0:T(8,128)(2,1)} %pad_maximum_fusion.1), calls=%async_computation | async-start | bytes 786432 | tf_op jit(solution)/shard_map/all_to_all | solution.py:65
  27.7 2.8 %copy-start.5 = (bf16[64,12,128]{2,1,0:T(8,128)(2,1)}, bf16[64,12,128]{2,1,0:T(8,128)(2,1)S(1)}, u32[]{:S(2)}) copy-start(bf16[64,12,128]{2,1,0:T(8,128)(2,1)S(1)} %select_n.42) | copy-start | bytes 589828
  27.7 2.8 %copy-start.3 = (f32[12,64,192]{2,1,0:T(8,128)S(1)}, f32[12,64,192]{2,1,0:T(8,128)}, u32[]{:S(2)}) copy-start(f32[12,64,192]{2,1,0:T(8,128)} %get-tuple-element.20) | copy-start | bytes 1769476
  33.3 1.0 copy-start.6
  103.0 1.1 copy-start.4
  105.5 1.9 %copy-start.1 = (bf16[2,64,1536]{2,1,0:T(8,128)(2,1)S(1)}, bf16[2,64,1536]{2,1,0:T(8,128)(2,1)}, u32[]{:S(2)}) copy-start(bf16[2,64,1536]{2,1,0:T(8,128)(2,1)} %constant_dynamic-update-slice_fusion.1) | copy-start | bytes 1179652
  107.5 9.1 %copy-start.2 = (bf16[2,64,1536]{2,1,0:T(8,128)(2,1)}, bf16[2,64,1536]{2,1,0:T(8,128)(2,1)S(1)}, u32[]{:S(2)}) copy-start(bf16[2,64,1536]{2,1,0:T(8,128)(2,1)S(1)} %constant_dynamic-update-slice_fusion) | copy-start | bytes 1179652
